TPU v7x, 128 devices: a whole 4x4x4 slice. The times are simulated.
128 devices in a mesh: row: 4 (over z), col: 32 (over x, y, core).
Axes of the slice: x: 4, y: 4, z: 4, core: 2. Of those that a mesh axis runs over, the one named last changes fastest.
Arguments:
- matrix_real: bfloat16 [512, 16384], P('col', 'row'), may hold values from -0.25 to 0.25
- matrix_imag: bfloat16 [512, 16384], P('col', 'row'), may hold values from -0.25 to 0.25
- valence_index: int32 [512], P('col'), may hold values from 0 to 15
- conduction_index: int32 [512], P('col'), may hold values from 0 to 31
- valence_energy: float32 [16], replicated, may hold values from -1.5 to -0.1
- conduction_energy: float32 [32], replicated, may hold values from 0.1 to 2
- frequency: float32 [2], replicated, may hold values from 0.2 to 2
Outputs:
- chi_real: bfloat16 [2, 16384, 16384], P(None, 'row', 'col')
- chi_imag: bfloat16 [2, 16384, 16384], P(None, 'row', 'col')
All inputs are finite; a program needn't handle non-finite values.
Results may differ from a plain program's by a relative error of at most 0.005.
Values may be sent and summed in bfloat16 or wider, within the bound.
No kernel may reach another device: no remote copies, remote signals or barrier semaphores. Data moves between devices by JAX's collectives and lax.ppermute only.
A program may use at most 192 MiB of HBM per device.

v0:
```python
import jax
import jax.numpy as jnp
from jax import lax
from jax.sharding import PartitionSpec as P


def lookup(indices, table):
    count = table.shape[0]
    picks = indices[:, None] == lax.broadcasted_iota(jnp.int32, (1, count), 1)
    return jnp.sum(jnp.where(picks, table[None, :], 0.0), axis=1)


def contract(left_side, right_side):
    return lax.dot_general(
        left_side, right_side, (((0,), (0,)), ((), ())), preferred_element_type=jnp.float32
    )


CHUNKS = 4


def on_device(
    matrix_real,
    matrix_imag,
    valence_index,
    conduction_index,
    valence_energy,
    conduction_energy,
    frequency,
):
    ncol = lax.psum(1, "col")
    local_pairs, local_g = matrix_real.shape
    pairs = local_pairs * ncol
    both = jnp.stack([matrix_real, matrix_imag])
    bands = jnp.stack([valence_index, conduction_index]).astype(jnp.float32)
    all_bands = lax.all_gather(bands, "col", axis=1, tiled=True).astype(jnp.int32)
    gap = lookup(all_bands[1], conduction_energy) - lookup(all_bands[0], valence_energy)
    spread = lax.all_gather(both, "row", axis=2, tiled=True)
    spread = spread.reshape(2, local_pairs, ncol, -1)
    column = lax.all_to_all(spread, "col", split_axis=2, concat_axis=1, tiled=True)
    width = column.shape[-1]
    wide = column.reshape(2, pairs, width).astype(jnp.float32)
    right_real = []
    right_imag = []
    for index in range(frequency.shape[0]):
        omega = frequency[index]
        weight = 4.0 * gap / (gap * gap + omega * omega)
        scaled_real = (weight[:, None] * wide[0]).astype(jnp.bfloat16)
        scaled_imag = (weight[:, None] * wide[1]).astype(jnp.bfloat16)
        right_real.append(jnp.concatenate([-scaled_real, -scaled_imag], axis=0))
        right_imag.append(jnp.concatenate([-scaled_imag, scaled_real], axis=0))
    step = local_g // CHUNKS
    real_parts = [[] for _ in right_real]
    imag_parts = [[] for _ in right_real]
    for chunk in range(CHUNKS):
        piece = both[:, :, chunk * step : (chunk + 1) * step]
        left = lax.all_gather(piece, "col", axis=1, tiled=True).reshape(2 * pairs, step)
        for index in range(len(right_real)):
            real_parts[index].append(contract(left, right_real[index]).astype(jnp.bfloat16))
            imag_parts[index].append(contract(left, right_imag[index]).astype(jnp.bfloat16))
    chi_real = jnp.stack([jnp.concatenate(p, axis=0) for p in real_parts])
    chi_imag = jnp.stack([jnp.concatenate(p, axis=0) for p in imag_parts])
    return (chi_real, chi_imag)


def solution(mesh):
    placed = (P("col", "row"), P("col", "row"), P("col"), P("col"), P(), P(), P())
    return jax.shard_map(
        on_device,
        mesh=mesh,
        in_specs=placed,
        out_specs=(P(None, "row", "col"), P(None, "row", "col")),
        check_vma=False,
    )
```

profile of v0, /device:TPU:1, one launch (start us, length us, event | category | flops | bytes accessed | tf_op | source)
XLA Modules:
  0.0 271.8 jit_solution(17406845412309366294)
XLA Ops:
  7.2 1.7 pad_maximum_fusion.6
  11.9 24.9 %all-gather.9.cloned.1.call-done = bf16[2,16,16384]{2,1,0:T(8,128)(2,1)} async-done(((bf16[2,16,4096]{2,1,0:T(8,128)(2,1)}), bf16[2,16,16384]{2,1,0:T(8,128)(2,1)}) %all-gather.9.cloned.1.call-update) | async-done | bytes 1048592 | tf_op jit(solution)/shard_map/all_gather | solution.py:38
  36.8 2.4 copy.26
  39.2 8.4 %all-to-all-start = ((bf16[2,16,32,512]{3,1,0,2:T(8,128)(2,1)}), bf16[2,16,32,512]{3,1,0,2:T(8,128)(2,1)S(1)}, u32[]{:S(2)}, u32[]{:S(2)}) async-start(bf16[2,16,32,512]{3,1,0,2:T(8,128)(2,1)} %bitcast.71), calls=%async_computation | async-start | bytes 2097152 | tf_op jit(solution)/shard_map/all_to_all | solution.py:40
  51.3 29.0 %all-gather = f32[32,16,2]{1,2,0:T(2,128)S(1)} all-gather(f32[1,16,2]{1,2,0:T(2,128)S(1)} %fusion.10), channel_id=1, replica_groups=mesh['row'=4,'col'=32] {'col'}, dimensions={0}, use_global_device_ids=true | all-gather | bytes 4224 | tf_op jit(solution)/shard_map/all_gather | solution.py:36
  82.7 5.7 %all-gather.11.cloned.1.call-done = bf16[2,512,1024]{2,1,0:T(8,128)(2,1)} async-done(((bf16[2,16,1024]{2,1,0:T(8,128)(2,1)}), bf16[2,512,1024]{2,1,0:T(8,128)(2,1)}) %all-gather.11.cloned.1.call-update) | async-done | bytes 2097168 | tf_op jit(solution)/shard_map/all_gather | solution.py:57
  88.4 3.8 %convolution_convert_fusion.10 = bf16[1024,512]{1,0:T(8,128)(2,1)} fusion(bf16[1024,1024]{1,0:T(8,128)(2,1)} %bitcast.82, bf16[512,512]{1,0:T(8,128)(2,1)S(1)} %get-tuple-element.11, bf16[512,512]{1,0:T(8,128)(2,1)S(1)} %get-tuple-element.16), kind=kOutput, calls=%fused_computation.17 | convolution fusion | flops 1076363264 | bytes 4194304 | tf_op jit(solution)/shard_map/dot_general | solution.py:14
  92.3 41.5 %all-gather.7.cloned.1.call-done = bf16[2,512,1024]{2,1,0:T(8,128)(2,1)} async-done(((bf16[2,16,1024]{2,1,0:T(8,128)(2,1)}), bf16[2,512,1024]{2,1,0:T(8,128)(2,1)}) %all-gather.7.cloned.1.call-update) | async-done | bytes 2097168 | tf_op jit(solution)/shard_map/all_gather | solution.py:57
  133.8 4.0 %convolution_convert_fusion.11 = bf16[1024,512]{1,0:T(8,128)(2,1)} fusion(bf16[1024,1024]{1,0:T(8,128)(2,1)} %bitcast.86, bf16[512,512]{1,0:T(8,128)(2,1)S(1)} %get-tuple-element.11, bf16[512,512]{1,0:T(8,128)(2,1)S(1)} %get-tuple-element.16), kind=kOutput, calls=%fused_computation.18 | convolution fusion | flops 1076363264 | bytes 4194304 | tf_op jit(solution)/shard_map/dot_general | solution.py:14
  139.3 2.5 convolution_convert_fusion.2
  141.9 37.1 %all-gather.13.cloned.1.call-done = bf16[2,512,1024]{2,1,0:T(8,128)(2,1)} async-done(((bf16[2,16,1024]{2,1,0:T(8,128)(2,1)}), bf16[2,512,1024]{2,1,0:T(8,128)(2,1)}) %all-gather.13.cloned.1.call-update) | async-done | bytes 2097168 | tf_op jit(solution)/shard_map/all_gather | solution.py:57
  179.0 4.2 %convolution_convert_fusion.9 = bf16[1024,512]{1,0:T(8,128)(2,1)} fusion(bf16[1024,1024]{1,0:T(8,128)(2,1)} %bitcast.90, bf16[512,512]{1,0:T(8,128)(2,1)} %copy-done.5, bf16[512,512]{1,0:T(8,128)(2,1)} %copy-done.11), kind=kOutput, calls=%fused_computation.16 | convolution fusion | flops 1076363264 | bytes 4194304 | tf_op jit(solution)/shard_map/dot_general | solution.py:14
  183.2 2.3 convolution_convert_fusion.1
  185.5 38.7 %all-gather.15.cloned.1.call-done = bf16[2,512,1024]{2,1,0:T(8,128)(2,1)} async-done(((bf16[2,16,1024]{2,1,0:T(8,128)(2,1)}), bf16[2,512,1024]{2,1,0:T(8,128)(2,1)}) %all-gather.15.cloned.1.call-update) | async-done | bytes 2097168 | tf_op jit(solution)/shard_map/all_gather | solution.py:57
  224.2 3.3 %convolution_convert_fusion.8 = bf16[1024,512]{1,0:T(8,128)(2,1)S(1)} fusion(bf16[1024,1024]{1,0:T(8,128)(2,1)} %bitcast.94, bf16[512,512]{1,0:T(8,128)(2,1)} %copy-done.5, bf16[512,512]{1,0:T(8,128)(2,1)} %copy-done.11), kind=kOutput, calls=%fused_computation.15 | convolution fusion | flops 1076363264 | bytes 4194304 | tf_op jit(solution)/shard_map/dot_general | solution.py:14
  227.5 2.3 convolution_convert_fusion
  232.7 2.5 convolution_convert_fusion.6
  235.2 2.3 convolution_convert_fusion.5
  238.8 2.4 convolution_convert_fusion.4
  241.2 2.3 convolution_convert_fusion.7
  245.3 2.8 %maximum_bitcast_fusion = (bf16[1,4096,512]{2,1,0:T(8,128)(2,1)S(1)}, bf16[1,4096,512]{2,1,0:T(8,128)(2,1)}) fusion(bf16[1024,512]{1,0:T(8,128)(2,1)S(1)} %convolution_convert_fusion.12, bf16[1024,512]{1,0:T(8,128)(2,1)S(1)} %convolution_convert_fusion.13, bf16[1024,512]{1,0:T(8,128)(2,1)S(1)} %convolution_convert_fusion.14, ...), kind=kLoop, calls=%fused_computation.2 | loop fusion | flops 33554432 | bytes 16777216 | tf_op jit(solution)/shard_map/stack | solution.py:61
  248.1 6.3 %pad_maximum_fusion = bf16[2,4096,512]{2,1,0:T(8,128)(2,1)} fusion(bf16[1,4096,512]{2,1,0:T(8,128)(2,1)} %get-tuple-element.27, bf16[1,4096,512]{2,1,0:T(8,128)(2,1)S(1)} %get-tuple-element.26), kind=kLoop, calls=%fused_computation | loop fusion | flops 4194304 | bytes 16777216 | tf_op jit(solution)/shard_map/stack | solution.py:61
  254.5 4.4 %maximum_bitcast_fusion.2 = (bf16[1,4096,512]{2,1,0:T(8,128)(2,1)S(1)}, bf16[1,4096,512]{2,1,0:T(8,128)(2,1)}) fusion(bf16[1024,512]{1,0:T(8,128)(2,1)} %convolution_convert_fusion.4, bf16[1024,512]{1,0:T(8,128)(2,1)} %convolution_convert_fusion.5, bf16[1024,512]{1,0:T(8,128)(2,1)} %convolution_convert_fusion.6, ...), kind=kLoop, calls=%fused_computation.4 | loop fusion | flops 33554432 | bytes 16777216 | tf_op jit(solution)/shard_map/stack | solution.py:62
  258.9 6.3 %pad_maximum_fusion.1 = bf16[2,4096,512]{2,1,0:T(8,128)(2,1)} fusion(bf16[1,4096,512]{2,1,0:T(8,128)(2,1)} %get-tuple-element.29, bf16[1,4096,512]{2,1,0:T(8,128)(2,1)S(1)} %get-tuple-element.28), kind=kLoop, calls=%fused_computation.1 | loop fusion | flops 4194304 | bytes 16777216 | tf_op jit(solution)/shard_map/stack | solution.py:62
  (78 shorter events, 14.1 us)
Async XLA Ops:
  7.2 29.6 %all-gather.9.cloned.1.call-start = ((), (), s32[]{:S(2)}) async-start(), calls=%async_computation.2 | async-start | bytes 1310720 | tf_op jit(solution)/shard_map/all_gather | solution.py:38
  8.9 79.5 %all-gather.11.cloned.1.call-start = ((), (), s32[]{:S(2)}) async-start(), calls=%async_computation.3 | async-start | bytes 2162688 | tf_op jit(solution)/shard_map/all_gather | solution.py:57
  10.6 123.2 %all-gather.7.cloned.1.call-start = ((), (), s32[]{:S(2)}) async-start(), calls=%async_computation.1 | async-start | bytes 2162688 | tf_op jit(solution)/shard_map/all_gather | solution.py:57
  11.3 167.7 %all-gather.13.cloned.1.call-start = ((), (), s32[]{:S(2)}) async-start(), calls=%async_computation.4 | async-start | bytes 2162688 | tf_op jit(solution)/shard_map/all_gather | solution.py:57
  36.8 11.5 %copy-start.12 = (f32[2]{0:T(128)S(1)}, f32[2]{0:T(128)}, u32[]{:S(2)}) copy-start(f32[2]{0:T(128)} %param.13) | copy-start | bytes 28
  36.8 14.5 %copy-start.15 = (s32[16]{0:T(128)S(1)}, s32[16]{0:T(128)}, u32[]{:S(2)}) copy-start(s32[16]{0:T(128)} %param.10) | copy-start | bytes 196
  36.8 14.5 %copy-start.16 = (s32[16]{0:T(128)S(1)}, s32[16]{0:T(128)}, u32[]{:S(2)}) copy-start(s32[16]{0:T(128)} %param.9) | copy-start | bytes 196
  36.8 43.8 %copy-start.13 = (f32[16]{0:T(128)S(1)}, f32[16]{0:T(128)}, u32[]{:S(2)}) copy-start(f32[16]{0:T(128)} %param.11) | copy-start | bytes 196
  36.8 43.9 %copy-start.14 = (f32[32]{0:T(128)S(1)}, f32[32]{0:T(128)}, u32[]{:S(2)}) copy-start(f32[32]{0:T(128)} %param.12) | copy-start | bytes 388
  39.2 41.6 %all-to-all-start = ((bf16[2,16,32,512]{3,1,0,2:T(8,128)(2,1)}), bf16[2,16,32,512]{3,1,0,2:T(8,128)(2,1)S(1)}, u32[]{:S(2)}, u32[]{:S(2)}) async-start(bf16[2,16,32,512]{3,1,0,2:T(8,128)(2,1)} %bitcast.71), calls=%async_computation | async-start | bytes 2097152 | tf_op jit(solution)/shard_map/all_to_all | solution.py:40
  47.6 176.6 %all-gather.15.cloned.1.call-start = ((), (), s32[]{:S(2)}) async-start(), calls=%async_computation.5 | async-start | bytes 2162688 | tf_op jit(solution)/shard_map/all_gather | solution.py:57
  82.7 51.0 %copy-start.11 = (bf16[512,512]{1,0:T(8,128)(2,1)}, bf16[512,512]{1,0:T(8,128)(2,1)S(1)}, u32[]{:S(2)}) copy-start(bf16[512,512]{1,0:T(8,128)(2,1)S(1)} %get-tuple-element.16) | copy-start | bytes 1572868
  82.7 55.0 %copy-start.5 = (bf16[512,512]{1,0:T(8,128)(2,1)}, bf16[512,512]{1,0:T(8,128)(2,1)S(1)}, u32[]{:S(2)}) copy-start(bf16[512,512]{1,0:T(8,128)(2,1)S(1)} %get-tuple-element.11) | copy-start | bytes 1572868
  82.7 55.0 %copy-start.8 = (bf16[512,512]{1,0:T(8,128)(2,1)}, bf16[512,512]{1,0:T(8,128)(2,1)S(1)}, u32[]{:S(2)}) copy-start(bf16[512,512]{1,0:T(8,128)(2,1)S(1)} %get-tuple-element.17) | copy-start | bytes 1572868
  133.7 4.0 %copy-start.19 = (bf16[2,512,1024]{2,1,0:T(8,128)(2,1)S(1)}, bf16[2,512,1024]{2,1,0:T(8,128)(2,1)}, u32[]{:S(2)}) copy-start(bf16[2,512,1024]{2,1,0:T(8,128)(2,1)} %all-gather.7.cloned.1.call-done) | copy-start | bytes 6291460
  179.0 4.2 %copy-start.6 = (bf16[512,512]{1,0:T(8,128)(2,1)S(1)}, bf16[512,512]{1,0:T(8,128)(2,1)}, u32[]{:S(2)}) copy-start(bf16[512,512]{1,0:T(8,128)(2,1)} %copy-done.5) | copy-start | bytes 1572868
  179.0 4.2 %copy-start.9 = (bf16[512,512]{1,0:T(8,128)(2,1)S(1)}, bf16[512,512]{1,0:T(8,128)(2,1)}, u32[]{:S(2)}) copy-start(bf16[512,512]{1,0:T(8,128)(2,1)} %copy-done.8) | copy-start | bytes 1572868
  179.0 4.2 %copy-start.21 = (bf16[2,512,1024]{2,1,0:T(8,128)(2,1)S(1)}, bf16[2,512,1024]{2,1,0:T(8,128)(2,1)}, u32[]{:S(2)}) copy-start(bf16[2,512,1024]{2,1,0:T(8,128)(2,1)} %all-gather.13.cloned.1.call-done) | copy-start | bytes 6291460
  224.2 3.3 %copy-start.7 = (bf16[512,512]{1,0:T(8,128)(2,1)S(1)}, bf16[512,512]{1,0:T(8,128)(2,1)}, u32[]{:S(2)}) copy-start(bf16[512,512]{1,0:T(8,128)(2,1)} %copy-done.5) | copy-start | bytes 1572868
  224.2 3.3 %copy-start.10 = (bf16[512,512]{1,0:T(8,128)(2,1)S(1)}, bf16[512,512]{1,0:T(8,128)(2,1)}, u32[]{:S(2)}) copy-start(bf16[512,512]{1,0:T(8,128)(2,1)} %copy-done.8) | copy-start | bytes 1572868
  224.2 3.3 %copy-start.23 = (bf16[2,512,1024]{2,1,0:T(8,128)(2,1)S(1)}, bf16[2,512,1024]{2,1,0:T(8,128)(2,1)}, u32[]{:S(2)}) copy-start(bf16[2,512,1024]{2,1,0:T(8,128)(2,1)} %all-gather.15.cloned.1.call-done) | copy-start | bytes 6291460
  227.5 2.3 copy-start.3
  227.5 2.3 copy-start.18
  238.8 2.4 copy-start.20
  (6 other events, 9.2 us)
Sparse Core Ops, SparseCore 0:
  10.2 26.4 all-gather.8
  39.7 48.6 all-gather.10
  90.8 42.9 all-gather.6
  136.0 42.9 all-gather.12
  181.2 42.9 all-gather.14
where the time goes:
time: 272 us
  waiting for transfers between devices  150 us (55%)
  matrix products  38.2 us (14%)
  blocking collectives  29 us (11%)
  other arithmetic  25.1 us (9%)
  between operations  16.5 us (6%)
  starting transfers between devices  8.64 us (3%)
  local copies, waits for them, and re-layouts  4.61 us (2%)
    all_gather x4, waiting for transfers between devices, on_device(): lax.all_gather(piece, 'col', axis=1, tiled=True).reshape(2 * pairs, step)  123 us
    dot_general x16, matrix products, contract(): lax.dot_general(left_side, right_side, (((0,), (0,)), ((), ())), preferre...  38.2 us
    all_gather x1, blocking collectives, on_device(): lax.all_gather(bands, 'col', axis=1, tiled=True).astype(jnp.int32)  29 us
    all_gather x1, waiting for transfers between devices, on_device(): spread = lax.all_gather(both, 'row', axis=2, tiled=True)  24.9 us
    another operation x2, other arithmetic, on_device(): chi_imag = jnp.stack([jnp.concatenate(p, axis=0) for p in imag_parts])  10.8 us
    another operation x2, other arithmetic, on_device(): chi_real = jnp.stack([jnp.concatenate(p, axis=0) for p in real_parts])  9.18 us
    all_to_all x1, starting transfers between devices, on_device(): lax.all_to_all(spread, 'col', split_axis=2, concat_axis=1, tiled=True)  8.44 us
  transfers between devices with their start and end apart: 6, of which 5 were waited for; matrix products, arithmetic and copies ran while one was open for 9% of the time, Pallas kernels for 0%

commit v1 on v0

--- a/solution.py
+++ b/solution.py
@@ -2,6 +2,17 @@
 import jax.numpy as jnp
 from jax import lax
 from jax.sharding import PartitionSpec as P
+
+
+def turned_line(x, axis, along):
+    count = lax.axis_size(axis)
+    right = [(i, (i + 1) % count) for i in range(count)]
+    pieces = [x]
+    for reach in range(1, count):
+        pieces = [lax.ppermute(pieces[0], axis, right), *pieces]
+    result = jnp.concatenate(pieces, axis=along)
+    offset = (lax.axis_index(axis) + 1) * pieces[-1].shape[along]
+    return jnp.roll(result, offset, axis=along)
 
 
 def lookup(indices, table):
@@ -35,7 +46,7 @@
     bands = jnp.stack([valence_index, conduction_index]).astype(jnp.float32)
     all_bands = lax.all_gather(bands, "col", axis=1, tiled=True).astype(jnp.int32)
     gap = lookup(all_bands[1], conduction_energy) - lookup(all_bands[0], valence_energy)
-    spread = lax.all_gather(both, "row", axis=2, tiled=True)
+    spread = turned_line(both, "row", 2)
     spread = spread.reshape(2, local_pairs, ncol, -1)
     column = lax.all_to_all(spread, "col", split_axis=2, concat_axis=1, tiled=True)
     width = column.shape[-1]

time: 272 us -> 250 us (0.919)
  waiting for transfers between devices: 150 us -> 124 us
  starting transfers between devices: 8.64 us -> 12.7 us
    all_gather x1 -> x0, waiting for transfers between devices: 24.9 us -> none  [on_device(): spread = lax.all_gather(both, 'row', axis=2, tiled=True)]
    all_gather x4, waiting for transfers between devices: 123 us -> 99.6 us  [on_device(): lax.all_gather(piece, 'col', axis=1, tiled=True).reshape(2 * pairs, step)]
    ppermute x0 -> x3, waiting for transfers between devices: none -> 22.9 us  [turned_line(): pieces = [lax.ppermute(pieces[0], axis, right), *pieces]]
  transfers between devices with their start and end apart: 6 -> 8, of which waited for: 5 -> 6; matrix products, arithmetic and copies ran while one was open for 9% -> 10% of each run, Pallas kernels for 0% -> 0%
where the time goes in v1:
time: 250 us
  waiting for transfers between devices  124 us (50%)
  matrix products  38.8 us (16%)
  blocking collectives  30 us (12%)
  other arithmetic  24.5 us (10%)
  between operations  16.4 us (7%)
  starting transfers between devices  12.7 us (5%)
  local copies, waits for them, and re-layouts  3.55 us (1%)
    all_gather x4, waiting for transfers between devices, on_device(): lax.all_gather(piece, 'col', axis=1, tiled=True).reshape(2 * pairs, step)  99.6 us
    dot_general x16, matrix products, contract(): lax.dot_general(left_side, right_side, (((0,), (0,)), ((), ())), preferre...  38.8 us
    all_gather x1, blocking collectives, on_device(): lax.all_gather(bands, 'col', axis=1, tiled=True).astype(jnp.int32)  30 us
    ppermute x3, waiting for transfers between devices, turned_line(): pieces = [lax.ppermute(pieces[0], axis, right), *pieces]  22.9 us
    another operation x2, other arithmetic, on_device(): chi_imag = jnp.stack([jnp.concatenate(p, axis=0) for p in imag_parts])  10.8 us
    all_to_all x1, starting transfers between devices, on_device(): lax.all_to_all(spread, 'col', split_axis=2, concat_axis=1, tiled=True)  10 us
    another operation x2, other arithmetic, on_device(): chi_real = jnp.stack([jnp.concatenate(p, axis=0) for p in real_parts])  9.18 us
  transfers between devices with their start and end apart: 8, of which 6 were waited for; matrix products, arithmetic and copies ran while one was open for 10% of the time, Pallas kernels for 0%

profile of v1, /device:TPU:1, one launch (start us, length us, event | category | flops | bytes accessed | tf_op | source)
XLA Modules:
  0.0 249.7 jit_solution(16800353719141102892)
XLA Ops:
  10.7 2.5 %collective-permute-start = (bf16[2,16,4096]{2,1,0:T(8,128)(2,1)S(1)}, bf16[2,16,4096]{2,1,0:T(8,128)(2,1)S(1)}, u32[]{:S(2)}, u32[]{:S(2)}) collective-permute-start(bf16[2,16,4096]{2,1,0:T(8,128)(2,1)S(1)} %pad_maximum_fusion.6), channel_id=1, source_target_pairs={{0,32},{32,64},{64,96},{96,0},{1,33},{33,65},{65,97},{97,1},{2,34}... | collective-permute-start | bytes 786440 | tf_op jit(solution)/shard_map/ppermute | solution.py:12
  13.2 8.2 %collective-permute-done = bf16[2,16,4096]{2,1,0:T(8,128)(2,1)S(1)} collective-permute-done((bf16[2,16,4096]{2,1,0:T(8,128)(2,1)S(1)}, bf16[2,16,4096]{2,1,0:T(8,128)(2,1)S(1)}, u32[]{:S(2)}, u32[]{:S(2)}) %collective-permute-start) | collective-permute-done | bytes 262176 | tf_op jit(solution)/shard_map/ppermute | solution.py:12
  21.4 7.8 %collective-permute-done.1 = bf16[2,16,4096]{2,1,0:T(8,128)(2,1)S(1)} collective-permute-done((bf16[2,16,4096]{2,1,0:T(8,128)(2,1)S(1)}, bf16[2,16,4096]{2,1,0:T(8,128)(2,1)S(1)}, u32[]{:S(2)}, u32[]{:S(2)}) %collective-permute-start.1) | collective-permute-done | bytes 262176 | tf_op jit(solution)/shard_map/ppermute | solution.py:12
  29.2 6.9 %collective-permute-done.2 = bf16[2,16,4096]{2,1,0:T(8,128)(2,1)S(1)} collective-permute-done((bf16[2,16,4096]{2,1,0:T(8,128)(2,1)S(1)}, bf16[2,16,4096]{2,1,0:T(8,128)(2,1)S(1)}, u32[]{:S(2)}, u32[]{:S(2)}) %collective-permute-start.2) | collective-permute-done | bytes 262176 | tf_op jit(solution)/shard_map/ppermute | solution.py:12
  37.7 10.0 %all-to-all-start = ((bf16[2,16,32,512]{3,1,0,2:T(8,128)(2,1)}), bf16[2,16,32,512]{3,1,0,2:T(8,128)(2,1)S(1)}, u32[]{:S(2)}, u32[]{:S(2)}) async-start(bf16[2,16,32,512]{3,1,0,2:T(8,128)(2,1)} %bitcast.71), calls=%async_computation | async-start | bytes 2097152 | tf_op jit(solution)/shard_map/all_to_all | solution.py:51
  51.1 30.0 %all-gather = f32[32,16,2]{1,2,0:T(2,128)S(1)} all-gather(f32[1,16,2]{1,2,0:T(2,128)S(1)} %fusion.10), channel_id=1, replica_groups=mesh['row'=4,'col'=32] {'col'}, dimensions={0}, use_global_device_ids=true | all-gather | bytes 4224 | tf_op jit(solution)/shard_map/all_gather | solution.py:47
  83.5 4.4 %convolution_convert_fusion.10 = bf16[1024,512]{1,0:T(8,128)(2,1)} fusion(bf16[1024,1024]{1,0:T(8,128)(2,1)} %bitcast.86, bf16[512,512]{1,0:T(8,128)(2,1)S(1)} %get-tuple-element.11, bf16[512,512]{1,0:T(8,128)(2,1)S(1)} %get-tuple-element.16), kind=kOutput, calls=%fused_computation.17 | convolution fusion | flops 1076363264 | bytes 4194304 | tf_op jit(solution)/shard_map/dot_general | solution.py:25
  87.9 23.6 %all-gather.6.cloned.1.call-done = bf16[2,512,1024]{2,1,0:T(8,128)(2,1)} async-done(((bf16[2,16,1024]{2,1,0:T(8,128)(2,1)}), bf16[2,512,1024]{2,1,0:T(8,128)(2,1)}) %all-gather.6.cloned.1.call-update) | async-done | bytes 2097168 | tf_op jit(solution)/shard_map/all_gather | solution.py:68
  111.5 4.0 %convolution_convert_fusion.11 = bf16[1024,512]{1,0:T(8,128)(2,1)} fusion(bf16[1024,1024]{1,0:T(8,128)(2,1)} %bitcast.90, bf16[512,512]{1,0:T(8,128)(2,1)S(1)} %get-tuple-element.11, bf16[512,512]{1,0:T(8,128)(2,1)S(1)} %get-tuple-element.16), kind=kOutput, calls=%fused_computation.18 | convolution fusion | flops 1076363264 | bytes 4194304 | tf_op jit(solution)/shard_map/dot_general | solution.py:25
  117.1 2.5 convolution_convert_fusion.2
  119.6 37.3 %all-gather.10.cloned.1.call-done = bf16[2,512,1024]{2,1,0:T(8,128)(2,1)} async-done(((bf16[2,16,1024]{2,1,0:T(8,128)(2,1)}), bf16[2,512,1024]{2,1,0:T(8,128)(2,1)}) %all-gather.10.cloned.1.call-update) | async-done | bytes 2097168 | tf_op jit(solution)/shard_map/all_gather | solution.py:68
  156.9 4.2 %convolution_convert_fusion.9 = bf16[1024,512]{1,0:T(8,128)(2,1)} fusion(bf16[1024,1024]{1,0:T(8,128)(2,1)} %bitcast.94, bf16[512,512]{1,0:T(8,128)(2,1)} %copy-done.7, bf16[512,512]{1,0:T(8,128)(2,1)} %copy-done.13), kind=kOutput, calls=%fused_computation.16 | convolution fusion | flops 1076363264 | bytes 4194304 | tf_op jit(solution)/shard_map/dot_general | solution.py:25
  161.1 2.3 convolution_convert_fusion.1
  163.4 38.7 %all-gather.12.cloned.1.call-done = bf16[2,512,1024]{2,1,0:T(8,128)(2,1)} async-done(((bf16[2,16,1024]{2,1,0:T(8,128)(2,1)}), bf16[2,512,1024]{2,1,0:T(8,128)(2,1)}) %all-gather.12.cloned.1.call-update) | async-done | bytes 2097168 | tf_op jit(solution)/shard_map/all_gather | solution.py:68
  202.1 3.3 %convolution_convert_fusion.8 = bf16[1024,512]{1,0:T(8,128)(2,1)S(1)} fusion(bf16[1024,1024]{1,0:T(8,128)(2,1)} %bitcast.98, bf16[512,512]{1,0:T(8,128)(2,1)} %copy-done.7, bf16[512,512]{1,0:T(8,128)(2,1)} %copy-done.13), kind=kOutput, calls=%fused_computation.15 | convolution fusion | flops 1076363264 | bytes 4194304 | tf_op jit(solution)/shard_map/dot_general | solution.py:25
  205.4 2.3 convolution_convert_fusion
  210.6 2.5 %convolution_convert_fusion.6 = bf16[1024,512]{1,0:T(8,128)(2,1)} fusion(bf16[1024,1024]{1,0:T(8,128)(2,1)S(1)} %bitcast.89, bf16[512,512]{1,0:T(8,128)(2,1)S(1)} %copy-done.6, bf16[512,512]{1,0:T(8,128)(2,1)S(1)} %get-tuple-element.10), kind=kOutput, calls=%fused_computation.13 | convolution fusion | flops 1076363264 | bytes 4194304 | tf_op jit(solution)/shard_map/dot_general | solution.py:25
  213.1 2.3 convolution_convert_fusion.5
  216.7 2.4 convolution_convert_fusion.4
  219.1 2.3 convolution_convert_fusion.7
  223.2 2.8 %maximum_bitcast_fusion = (bf16[1,4096,512]{2,1,0:T(8,128)(2,1)S(1)}, bf16[1,4096,512]{2,1,0:T(8,128)(2,1)}) fusion(bf16[1024,512]{1,0:T(8,128)(2,1)S(1)} %convolution_convert_fusion.12, bf16[1024,512]{1,0:T(8,128)(2,1)S(1)} %convolution_convert_fusion.13, bf16[1024,512]{1,0:T(8,128)(2,1)S(1)} %convolution_convert_fusion.14, ...), kind=kLoop, calls=%fused_computation.2 | loop fusion | flops 33554432 | bytes 16777216 | tf_op jit(solution)/shard_map/stack | solution.py:72
  226.0 6.3 %pad_maximum_fusion = bf16[2,4096,512]{2,1,0:T(8,128)(2,1)} fusion(bf16[1,4096,512]{2,1,0:T(8,128)(2,1)} %get-tuple-element.27, bf16[1,4096,512]{2,1,0:T(8,128)(2,1)S(1)} %get-tuple-element.26), kind=kLoop, calls=%fused_computation | loop fusion | flops 4194304 | bytes 16777216 | tf_op jit(solution)/shard_map/stack | solution.py:72
  232.4 4.4 %maximum_bitcast_fusion.2 = (bf16[1,4096,512]{2,1,0:T(8,128)(2,1)S(1)}, bf16[1,4096,512]{2,1,0:T(8,128)(2,1)}) fusion(bf16[1024,512]{1,0:T(8,128)(2,1)} %convolution_convert_fusion.4, bf16[1024,512]{1,0:T(8,128)(2,1)} %convolution_convert_fusion.5, bf16[1024,512]{1,0:T(8,128)(2,1)} %convolution_convert_fusion.6, ...), kind=kLoop, calls=%fused_computation.4 | loop fusion | flops 33554432 | bytes 16777216 | tf_op jit(solution)/shard_map/stack | solution.py:73
  236.8 6.3 %pad_maximum_fusion.1 = bf16[2,4096,512]{2,1,0:T(8,128)(2,1)} fusion(bf16[1,4096,512]{2,1,0:T(8,128)(2,1)} %get-tuple-element.29, bf16[1,4096,512]{2,1,0:T(8,128)(2,1)S(1)} %get-tuple-element.28), kind=kLoop, calls=%fused_computation.1 | loop fusion | flops 4194304 | bytes 16777216 | tf_op jit(solution)/shard_map/stack | solution.py:73
  (94 shorter events, 16.0 us)
Async XLA Ops:
  7.2 29.1 %copy-start.1 = (bf16[16,4096]{1,0:T(8,128)(2,1)S(1)}, bf16[16,4096]{1,0:T(8,128)(2,1)}, u32[]{:S(2)}) copy-start(bf16[16,4096]{1,0:T(8,128)(2,1)} %param.8) | copy-start | bytes 393220
  7.2 29.1 %copy-start = (bf16[16,4096]{1,0:T(8,128)(2,1)S(1)}, bf16[16,4096]{1,0:T(8,128)(2,1)}, u32[]{:S(2)}) copy-start(bf16[16,4096]{1,0:T(8,128)(2,1)} %param.7) | copy-start | bytes 393220
  7.2 76.3 %all-gather.8.cloned.1.call-start = ((), (), s32[]{:S(2)}) async-start(), calls=%async_computation.2 | async-start | bytes 2162688 | tf_op jit(solution)/shard_map/all_gather | solution.py:68
  8.9 102.6 %all-gather.6.cloned.1.call-start = ((), (), s32[]{:S(2)}) async-start(), calls=%async_computation.1 | async-start | bytes 2162688 | tf_op jit(solution)/shard_map/all_gather | solution.py:68
  9.6 147.2 %all-gather.10.cloned.1.call-start = ((), (), s32[]{:S(2)}) async-start(), calls=%async_computation.3 | async-start | bytes 2162688 | tf_op jit(solution)/shard_map/all_gather | solution.py:68
  10.7 10.7 %collective-permute-start = (bf16[2,16,4096]{2,1,0:T(8,128)(2,1)S(1)}, bf16[2,16,4096]{2,1,0:T(8,128)(2,1)S(1)}, u32[]{:S(2)}, u32[]{:S(2)}) collective-permute-start(bf16[2,16,4096]{2,1,0:T(8,128)(2,1)S(1)} %pad_maximum_fusion.6), channel_id=1, source_target_pairs={{0,32},{32,64},{64,96},{96,0},{1,33},{33,65},{65,97},{97,1},{2,34}... | collective-permute-start | bytes 786440 | tf_op jit(solution)/shard_map/ppermute | solution.py:12
  21.4 7.8 %collective-permute-start.1 = (bf16[2,16,4096]{2,1,0:T(8,128)(2,1)S(1)}, bf16[2,16,4096]{2,1,0:T(8,128)(2,1)S(1)}, u32[]{:S(2)}, u32[]{:S(2)}) collective-permute-start(bf16[2,16,4096]{2,1,0:T(8,128)(2,1)S(1)} %collective-permute-done), channel_id=1, source_target_pairs={{0,32},{32,64},{64,96},{96,0},{1,33},{33,65},{65,97},{97,1},{2,34}... | collective-permute-start | bytes 786440 | tf_op jit(solution)/shard_map/ppermute | solution.py:12
  29.2 7.0 %collective-permute-start.2 = (bf16[2,16,4096]{2,1,0:T(8,128)(2,1)S(1)}, bf16[2,16,4096]{2,1,0:T(8,128)(2,1)S(1)}, u32[]{:S(2)}, u32[]{:S(2)}) collective-permute-start(bf16[2,16,4096]{2,1,0:T(8,128)(2,1)S(1)} %collective-permute-done.1), channel_id=1, source_target_pairs={{0,32},{32,64},{64,96},{96,0},{1,33},{33,65},{65,97},{97,1},{2,34}... | collective-permute-start | bytes 786440 | tf_op jit(solution)/shard_map/ppermute | solution.py:12
  36.5 11.8 %copy-start.14 = (f32[2]{0:T(128)S(1)}, f32[2]{0:T(128)}, u32[]{:S(2)}) copy-start(f32[2]{0:T(128)} %param.13) | copy-start | bytes 28
  36.5 14.6 %copy-start.17 = (s32[16]{0:T(128)S(1)}, s32[16]{0:T(128)}, u32[]{:S(2)}) copy-start(s32[16]{0:T(128)} %param.10) | copy-start | bytes 196
  36.5 14.6 %copy-start.18 = (s32[16]{0:T(128)S(1)}, s32[16]{0:T(128)}, u32[]{:S(2)}) copy-start(s32[16]{0:T(128)} %param.9) | copy-start | bytes 196
  36.5 44.9 %copy-start.15 = (f32[16]{0:T(128)S(1)}, f32[16]{0:T(128)}, u32[]{:S(2)}) copy-start(f32[16]{0:T(128)} %param.11) | copy-start | bytes 196
  36.5 45.0 %copy-start.16 = (f32[32]{0:T(128)S(1)}, f32[32]{0:T(128)}, u32[]{:S(2)}) copy-start(f32[32]{0:T(128)} %param.12) | copy-start | bytes 388
  37.7 43.9 %all-to-all-start = ((bf16[2,16,32,512]{3,1,0,2:T(8,128)(2,1)}), bf16[2,16,32,512]{3,1,0,2:T(8,128)(2,1)S(1)}, u32[]{:S(2)}, u32[]{:S(2)}) async-start(bf16[2,16,32,512]{3,1,0,2:T(8,128)(2,1)} %bitcast.71), calls=%async_computation | async-start | bytes 2097152 | tf_op jit(solution)/shard_map/all_to_all | solution.py:51
  47.7 154.4 %all-gather.12.cloned.1.call-start = ((), (), s32[]{:S(2)}) async-start(), calls=%async_computation.4 | async-start | bytes 2162688 | tf_op jit(solution)/shard_map/all_gather | solution.py:68
  83.5 28.0 %copy-start.13 = (bf16[512,512]{1,0:T(8,128)(2,1)}, bf16[512,512]{1,0:T(8,128)(2,1)S(1)}, u32[]{:S(2)}) copy-start(bf16[512,512]{1,0:T(8,128)(2,1)S(1)} %get-tuple-element.16) | copy-start | bytes 1572868
  83.5 32.0 %copy-start.7 = (bf16[512,512]{1,0:T(8,128)(2,1)}, bf16[512,512]{1,0:T(8,128)(2,1)S(1)}, u32[]{:S(2)}) copy-start(bf16[512,512]{1,0:T(8,128)(2,1)S(1)} %get-tuple-element.11) | copy-start | bytes 1572868
  83.5 32.0 %copy-start.10 = (bf16[512,512]{1,0:T(8,128)(2,1)}, bf16[512,512]{1,0:T(8,128)(2,1)S(1)}, u32[]{:S(2)}) copy-start(bf16[512,512]{1,0:T(8,128)(2,1)S(1)} %get-tuple-element.17) | copy-start | bytes 1572868
  111.5 4.0 %copy-start.21 = (bf16[2,512,1024]{2,1,0:T(8,128)(2,1)S(1)}, bf16[2,512,1024]{2,1,0:T(8,128)(2,1)}, u32[]{:S(2)}) copy-start(bf16[2,512,1024]{2,1,0:T(8,128)(2,1)} %all-gather.6.cloned.1.call-done) | copy-start | bytes 6291460
  156.9 4.2 %copy-start.8 = (bf16[512,512]{1,0:T(8,128)(2,1)S(1)}, bf16[512,512]{1,0:T(8,128)(2,1)}, u32[]{:S(2)}) copy-start(bf16[512,512]{1,0:T(8,128)(2,1)} %copy-done.7) | copy-start | bytes 1572868
  156.9 4.2 %copy-start.11 = (bf16[512,512]{1,0:T(8,128)(2,1)S(1)}, bf16[512,512]{1,0:T(8,128)(2,1)}, u32[]{:S(2)}) copy-start(bf16[512,512]{1,0:T(8,128)(2,1)} %copy-done.10) | copy-start | bytes 1572868
  156.9 4.2 %copy-start.23 = (bf16[2,512,1024]{2,1,0:T(8,128)(2,1)S(1)}, bf16[2,512,1024]{2,1,0:T(8,128)(2,1)}, u32[]{:S(2)}) copy-start(bf16[2,512,1024]{2,1,0:T(8,128)(2,1)} %all-gather.10.cloned.1.call-done) | copy-start | bytes 6291460
  202.1 3.3 %copy-start.12 = (bf16[512,512]{1,0:T(8,128)(2,1)S(1)}, bf16[512,512]{1,0:T(8,128)(2,1)}, u32[]{:S(2)}) copy-start(bf16[512,512]{1,0:T(8,128)(2,1)} %copy-done.10) | copy-start | bytes 1572868
  202.1 3.3 %copy-start.25 = (bf16[2,512,1024]{2,1,0:T(8,128)(2,1)S(1)}, bf16[2,512,1024]{2,1,0:T(8,128)(2,1)}, u32[]{:S(2)}) copy-start(bf16[2,512,1024]{2,1,0:T(8,128)(2,1)} %all-gather.12.cloned.1.call-done) | copy-start | bytes 6291460
  (10 other events, 19.4 us)
Sparse Core Ops, SparseCore 0:
  11.0 52.8 all-gather.7
  66.3 45.1 all-gather.5
  113.9 42.9 all-gather.9
  159.1 42.9 all-gather.11
